TPU v7x, 128 devices: a whole 4x4x4 slice. The times are simulated.
128 devices in a mesh: tm: 32 (over x, z, core), sub: 4 (over y).
Axes of the slice: x: 4, y: 4, z: 4, core: 2. Of those that a mesh axis runs over, the one named last changes fastest.
Arguments:
- vis_coords: float32 [16384, 2, 1024], P(('tm', 'sub')), may hold values from 0 to 31
- vis_values: float32 [16384, 2, 1024], P(('tm', 'sub')), may hold values from -1.6 to 1.6
- block_dest: int32 [16384, 1], P(('tm', 'sub')), may hold values from 0 to 127; in each aligned block of 128 rows (0 to 127, 128 to 255, ...) at most 2 rows name the same one
- block_local: int32 [16384], P(('tm', 'sub')), may hold values from 0 to 15
- block_tile: int32 [16384], P(('tm', 'sub')), may hold values from 0 to 63
- block_counts: int32 [128], P(('tm', 'sub')), may hold values from 64 to 128, as said below
- facet_offsets: int32 [32, 2], replicated, may hold values from 0 to 384
- correction: float32 [32, 128, 128], P('tm', 'sub'), may hold values from 0.2 to 2
Outputs:
- facets: float32 [32, 128, 2, 128], P('tm', 'sub')
Inputs may be any that keep to these rules, and one draw needn't show every extreme that they name: `block_dest`: among the 128 blocks of one device at most 2 name the same destination, a bound that some device reaches. `block_counts`: some device's count is 128.
All inputs are finite; a program needn't handle non-finite values.
Results may differ from a plain program's by a relative error of at most 0.000096.
Values sent between devices are 32-bit elements; how exact they have to be, the bound alone decides.
No kernel may reach another device: no remote copies, remote signals or barrier semaphores. Data moves between devices by JAX's collectives and lax.ppermute only.
A program may use at most 128 MiB of HBM per device.

v0:
```python
import math

import jax
import jax.numpy as jnp
from jax import lax
from jax.sharding import PartitionSpec as P

SG = 512
PATCH = 32
FS = 128
VIS = 1024
SG_PER = 16


kernel_width = 0.7


def make_patches(vis_coords, vis_values):
    count = vis_coords.shape[0]
    group = math.gcd(count, 16)
    cells = jnp.arange(PATCH).astype(jnp.float32)

    def one_group(pieces):
        coords, values = pieces
        rows_kernel = jnp.exp(
            -0.5 * ((coords[:, 0, None, :] - cells[None, :, None]) / kernel_width) ** 2
        )
        cols_kernel = jnp.exp(
            -0.5 * ((coords[:, 1, None, :] - cells[None, :, None]) / kernel_width) ** 2
        )
        weighted = values[:, :, None, :] * cols_kernel[:, None, :, :]
        patch = jnp.einsum("nak,npbk->napb", rows_kernel, weighted, precision=lax.Precision.HIGHEST)
        return patch.reshape(group, 2 * PATCH * PATCH)

    shaped = (
        vis_coords.reshape(count // group, group, 2, VIS),
        vis_values.reshape(count // group, group, 2, VIS),
    )
    return lax.map(one_group, shaped).reshape(count, 2 * PATCH * PATCH)


def column_table():
    index = jnp.arange(SG, dtype=jnp.int32)
    phase = index[:, None] * index[None, :] % SG
    angle = phase.astype(jnp.float32) * (2.0 * math.pi / SG)
    scale = 1.0 / math.sqrt(SG)
    cosine = jnp.cos(angle) * scale
    sine = jnp.sin(angle) * scale
    return jnp.concatenate(
        [jnp.concatenate([cosine, -sine], 1), jnp.concatenate([sine, cosine], 1)], 0
    )


def row_table(first_row, count):
    ys = jnp.arange(SG, dtype=jnp.int32)
    rows = first_row + jnp.arange(count, dtype=jnp.int32)
    phase = ys[:, None] * rows[None, :] % SG
    angle = phase.astype(jnp.float32) * (2.0 * math.pi / SG)
    scale = 1.0 / math.sqrt(SG)
    return jnp.concatenate([jnp.cos(angle) * scale, -jnp.sin(angle) * scale], 1)


def facet_terms(spectrum, table, offsets):
    stride = SG // SG_PER
    total = spectrum[0]
    for local in range(1, SG_PER):
        total = total + jnp.roll(spectrum[local], -local * stride, axis=2)

    def one_facet(offset):
        left = lax.dynamic_slice_in_dim(table, offset[0], FS, 0)
        window = lax.dynamic_slice_in_dim(total, offset[1], FS, 2)
        real_part = window[:, 0]
        imag_part = window[:, 1]
        right = jnp.concatenate(
            [
                jnp.concatenate([real_part, imag_part], 1),
                jnp.concatenate([-imag_part, real_part], 1),
            ],
            0,
        )
        return jnp.dot(left, right, precision=lax.Precision.HIGHEST)

    return lax.map(one_facet, offsets)


def body(
    vis_coords,
    vis_values,
    block_dest,
    block_local,
    block_tile,
    block_counts,
    facet_offsets,
    correction,
):
    n_tm = lax.axis_size("tm")
    n_sub = lax.axis_size("sub")
    devices = n_tm * n_sub
    blocks = vis_coords.shape[0]
    capacity = max(2, 2 * blocks // devices)
    band_rows = SG // n_sub
    band_tiles = band_rows // PATCH
    col_tiles = SG // PATCH
    tile_count = band_tiles * col_tiles
    grids_here = SG_PER
    facet_count = facet_offsets.shape[0]
    patch_size = 2 * PATCH * PATCH
    patches = make_patches(vis_coords, vis_values)
    live_block = jnp.arange(blocks, dtype=jnp.int32) < block_counts[0]
    target = block_dest[:, 0]
    hits = (
        (target[:, None] == jnp.arange(devices, dtype=jnp.int32)[None, :]) & live_block[:, None]
    ).astype(jnp.int32)
    earlier = jnp.cumsum(hits, axis=0) - hits
    arrival = jnp.sum(earlier * hits, axis=1)
    slot_index = jnp.where(live_block, target * capacity + arrival, -1)
    chooser = slot_index[None, :] == jnp.arange(devices * capacity, dtype=jnp.int32)[:, None]
    outgoing = jnp.dot(chooser.astype(jnp.float32), patches, precision=lax.Precision.HIGHEST)
    tile_code = block_local * tile_count + block_tile + 1
    out_codes = jnp.sum(jnp.where(chooser, tile_code[None, :], 0), axis=1)
    arrived, codes = (
        lax.all_to_all(
            outgoing.reshape(devices, capacity, patch_size),
            ("tm", "sub"),
            split_axis=0,
            concat_axis=0,
            tiled=True,
        ),
        lax.all_to_all(
            out_codes.reshape(devices, capacity),
            ("tm", "sub"),
            split_axis=0,
            concat_axis=0,
            tiled=True,
        ),
    )
    arrived = arrived.reshape(devices * capacity, patch_size)
    codes = codes.reshape(devices * capacity)
    placer = (
        codes[None, :] - 1 == jnp.arange(grids_here * tile_count, dtype=jnp.int32)[:, None]
    ).astype(jnp.float32)
    tiles = jnp.dot(placer, arrived, precision=lax.Precision.HIGHEST)
    grid = (
        tiles.reshape(grids_here, band_tiles, col_tiles, PATCH, 2, PATCH)
        .transpose(0, 1, 3, 4, 2, 5)
        .reshape(grids_here * band_rows, 2 * SG)
    )
    spectrum = jnp.dot(grid, column_table(), precision=lax.Precision.HIGHEST).reshape(
        grids_here, band_rows, 2, SG
    )
    table = row_table(lax.axis_index("sub") * band_rows, band_rows)
    terms = facet_terms(spectrum, table, facet_offsets)
    facet_rows = FS // n_sub
    summed = lax.psum_scatter(
        terms.reshape(facet_count * n_sub, facet_rows, 2, FS),
        ("tm", "sub"),
        scatter_dimension=0,
        tiled=True,
    )
    return summed * correction[:, :, None, :]


def solution(mesh):
    in_specs = (
        P(("tm", "sub"), None, None),
        P(("tm", "sub"), None, None),
        P(("tm", "sub"), None),
        P(("tm", "sub")),
        P(("tm", "sub")),
        P(("tm", "sub")),
        P(),
        P("tm", "sub", None),
    )
    out_specs = P("tm", "sub", None, None)
    return jax.shard_map(body, mesh=mesh, in_specs=in_specs, out_specs=out_specs, check_vma=False)
```

profile of v0, /device:TPU:1, one launch (start us, length us, event | category | flops | bytes accessed | tf_op | source)
XLA Modules:
  0.0 1193.9 jit_solution(13971609099531257522)
XLA Ops:
  10.6 11.5 all-to-all-start
  22.1 107.5 %while.23 = (s32[]{:T(128)}, f32[8,16,2048]{2,1,0:T(8,128)S(1)}, f32[8,16,2,1024]{3,2,1,0:T(2,128)}, f32[8,16,2,1024]{3,2,1,0:T(2,128)}, s32[]{:T(128)}) while((s32[]{:T(128)}, f32[8,16,2048]{2,1,0:T(8,128)S(1)}, f32[8,16,2,1024]{3,2,1,0:T(2,128)}, f32[8,16,2,1024]{3,2,1,0:T(2,128)}, s32[]{:T(128)}) %tuple.78), condition=%wide.region_4.5_spmd.clone.clone, body=%wide.region_3.4_spmd.clone.clone.sunk | while | flops 407896096 | bytes 6422985 | solution.py:39
  24.5 9.9 fusion.92
  37.9 9.9 fusion.92
  51.4 9.9 fusion.92
  64.8 9.9 fusion.92
  78.2 9.9 fusion.92
  91.7 9.9 fusion.92
  105.1 9.9 fusion.92
  118.5 9.9 fusion.92
  130.6 3.0 copy.162
  133.5 9.8 all-to-all-start.1
  145.5 3.9 fusion.59
  149.3 5.0 sine_multiply_fusion
  154.7 19.6 %all-to-all-done.1 = f32[128,2,2048]{2,1,0:T(2,128)S(1)} async-done(((f32[128,2,2048]{2,1,0:T(2,128)}), f32[128,2,2048]{2,1,0:T(2,128)S(1)}, u32[]{:S(2)}, u32[]{:S(2)}) %all-to-all-start.1) | async-done | bytes 2097184 | tf_op jit(solution)/shard_map/all_to_all | solution.py:122
  174.3 2.4 reshape.150
  176.7 1.9 copy.163
  178.7 17.3 %convolution_bitcast_fusion.1 = f32[16,4,32,2,16,32]{5,4,3,2,1,0:T(8,128)} fusion(f32[32,2,32,256,1,1]{3,2,1,0,5,4:T(8,128)S(1)} %bitcast.89, s32[16,4,16]{2,1,0:T(4,128)S(1)} %multiply_add_fusion, s32[256]{0:T(256)S(1)} %sub.45), kind=kOutput, calls=%fused_computation.40 | convolution fusion | flops 6442713088 | bytes 10490880 | tf_op jit(solution)/shard_map/dot_general | solution.py:142
  195.9 26.2 %reshape.151 = f32[2048,1024]{1,0:T(8,128)} reshape(f32[16,4,32,2,16,32]{5,4,3,2,1,0:T(8,128)} %convolution_bitcast_fusion.1) | data formatting | bytes 16777216 | tf_op jit(solution)/shard_map/reshape | solution.py:146
  222.2 31.9 %fusion.29 = f32[2048,1024]{0,1:T(8,128)S(1)} fusion(f32[2048,1024]{1,0:T(8,128)} %reshape.151, f32[512,512]{1,0:T(8,128)S(1)} %copy-done.3, f32[512,512]{1,0:T(8,128)S(1)} %copy-done.2, f32[512,512]{1,0:T(8,128)S(1)} %fusion.59), kind=kOutput, calls=%fused_computation.41 | convolution fusion | flops 25772949504 | bytes 19922944 | tf_op jit(solution)/shard_map/dot_general | solution.py:148
  273.2 2.0 copy.206
  275.2 2.0 copy.231
  284.3 1.9 copy.210
  286.2 1.9 copy.227
  288.1 1.9 copy.212
  291.9 1.9 copy.223
  293.8 1.9 copy.216
  314.5 7.5 fusion.56
  322.1 221.0 %while.22 = (s32[]{:T(128)}, f32[32,128,256]{2,1,0:T(8,128)}, s32[32,2]{0,1:T(2,128)S(1)}, f32[512,256]{1,0:T(8,128)}, f32[128,2,512]{2,1,0:T(2,128)S(1)}, /*index=5*/s32[]{:T(128)}, s32[]{:T(128)}, s32[]{}, s32[]{:T(128)}) while((s32[]{:T(128)}, f32[32,128,256]{2,1,0:T(8,128)}, s32[32,2]{0,1:T(2,128)S(1)}, f32[512,256]{1,0:T(8,128)}, ...), condition=%wide.region_6.7_spmd, body=%wide.region_5.6_spmd.sunk | while | flops 100876296 | bytes 852701 | solution.py:83
  543.1 5.8 reshape.152
  548.9 4.8 copy.195
  553.6 631.6 %reduce-scatter.2.cloned.1.call-done = f32[1,32,2,128]{3,1,2,0:T(8,128)} async-done(((f32[128,32,2,128]{3,1,2,0:T(8,128)}), f32[1,32,2,128]{3,1,2,0:T(8,128)}) %reduce-scatter.2.cloned.1.call-update) | async-done | bytes 32784 | tf_op jit(solution)/shard_map/reduce_scatter | solution.py:154
  (332 shorter events, 174.9 us)
Async XLA Ops:
  10.6 123.0 %all-to-all-start = ((s32[128,1,2]{2,1,0:T(1,128)}), s32[128,1,2]{2,1,0:T(1,128)S(1)}, u32[]{:S(2)}, u32[]{:S(2)}) async-start(s32[128,1,2]{2,1,0:T(1,128)} %bitcast.7), calls=%async_computation | async-start | bytes 131072 | tf_op jit(solution)/shard_map/all_to_all | solution.py:129
  133.5 40.8 %all-to-all-start.1 = ((f32[128,2,2048]{2,1,0:T(2,128)}), f32[128,2,2048]{2,1,0:T(2,128)S(1)}, u32[]{:S(2)}, u32[]{:S(2)}) async-start(f32[128,2,2048]{2,1,0:T(2,128)} %copy.162), calls=%async_computation.1 | async-start | bytes 4194304 | tf_op jit(solution)/shard_map/all_to_all | solution.py:122
  143.3 1041.9 %reduce-scatter.2.cloned.1.call-start = ((), (), s32[]{:S(2)}) async-start(), calls=%async_computation.3 | async-start | bytes 4227072 | tf_op jit(solution)/shard_map/reduce_scatter | solution.py:154
  195.9 26.2 %copy-start.2 = (f32[512,512]{1,0:T(8,128)S(1)}, f32[512,512]{1,0:T(8,128)}, u32[]{:S(2)}) copy-start(f32[512,512]{1,0:T(8,128)} %get-tuple-element.150) | copy-start | bytes 3145732
  195.9 26.2 %copy-start.3 = (f32[512,512]{1,0:T(8,128)S(1)}, f32[512,512]{1,0:T(8,128)}, u32[]{:S(2)}) copy-start(f32[512,512]{1,0:T(8,128)} %get-tuple-element.151) | copy-start | bytes 3145732
  280.6 9.4 copy-start
  291.0 4.7 copy-start.1
  291.0 7.5 copy-start.4
  295.7 14.8 %copy-start.7 = (f32[128,2,64]{0,2,1:T(8,128)S(1)}, f32[128,2,64]{0,2,1:T(8,128)}, u32[]{:S(2)}) copy-start(f32[128,2,64]{0,2,1:T(8,128)} %slice.262) | copy-start | bytes 196612
  296.6 7.3 copy-start.5
  296.6 11.4 copy-start.6
  296.6 14.6 %copy-start.8 = (f32[128,2,64]{0,2,1:T(8,128)S(1)}, f32[128,2,64]{0,2,1:T(8,128)}, u32[]{:S(2)}) copy-start(f32[128,2,64]{0,2,1:T(8,128)} %slice.297) | copy-start | bytes 196612
  296.6 15.3 %copy-start.9 = (f32[128,2,32]{0,2,1:T(8,128)S(1)}, f32[128,2,32]{0,2,1:T(8,128)}, u32[]{:S(2)}) copy-start(f32[128,2,32]{0,2,1:T(8,128)} %slice.259) | copy-start | bytes 98308
  314.5 7.6 copy-start.10
  553.6 631.6 %copy-start.11 = (f32[1,32,128]{2,1,0:T(8,128)S(1)}, f32[1,32,128]{2,1,0:T(8,128)}, u32[]{:S(2)}) copy-start(f32[1,32,128]{2,1,0:T(8,128)} %param.19) | copy-start | bytes 49156
Sparse Core Ops, SparseCore 0:
  553.8 631.4 reduce-scatter.1
where the time goes:
time: 1210 us; the launch traced here: 1190 us
  waiting for transfers between devices  651 us (54%)
  matrix products  189 us (16%)
  local copies, waits for them, and re-layouts  162 us (13%)
  loops' own time  130 us (11%)
  other arithmetic  26 us (2%)
  starting transfers between devices  21.5 us (2%)
  between operations  14.7 us (1%)
    reduce_scatter x1, waiting for transfers between devices, body(): lax.psum_scatter(terms.reshape(facet_count * n_sub, facet_rows, 2, FS), (...  632 us
    another operation x1, loops' own time, facet_terms(): return lax.map(one_facet, offsets)  129 us
    dot_general x8, matrix products, one_group(): jnp.einsum('nak,npbk->napb', rows_kernel, weighted, precision=lax.Precisi...  79.1 us
    dot_general x32, matrix products, one_facet(): return jnp.dot(left, right, precision=lax.Precision.HIGHEST)  59.4 us
    unnamed x54, local copies, waits for them, and re-layouts  40.6 us
    dot_general x1, matrix products, body(): jnp.dot(grid, column_table(), precision=lax.Precision.HIGHEST)  31.9 us
    reshape x1, local copies, waits for them, and re-layouts, body(): grid = tiles.reshape(grids_here, band_tiles, col_tiles, PATCH, 2, PATCH)....  26.2 us
  transfers between devices with their start and end apart: 3, of which 2 were waited for; matrix products, arithmetic and copies ran while one was open for 10% of the time, Pallas kernels for 0%

commit v1 on v0

v1 whole, which is shorter than its diff:
```python
import math

import jax
import jax.numpy as jnp
from jax import lax
from jax.sharding import PartitionSpec as P

SG = 512
PATCH = 32
FS = 128
VIS = 1024
SG_PER = 16


kernel_width = 0.7


def make_phased_patches(vis_coords, vis_values, live, local):
    count = vis_coords.shape[0]
    cells = jnp.arange(PATCH, dtype=jnp.float32)
    rows_kernel = jnp.exp(
        -0.5 * ((vis_coords[:, 0, None, :] - cells[None, :, None]) / kernel_width) ** 2
    )
    cols_kernel = jnp.exp(
        -0.5 * ((vis_coords[:, 1, None, :] - cells[None, :, None]) / kernel_width) ** 2
    )
    values = jnp.where(live[:, None, None], vis_values, 0.0)
    phase = (jnp.arange(PATCH, dtype=jnp.int32)[None, :] * local[:, None]) % SG_PER
    angle = phase.astype(jnp.float32) * (2.0 * math.pi / SG_PER)
    cos_b = jnp.cos(angle)[:, :, None]
    sin_b = jnp.sin(angle)[:, :, None]
    v_re = values[:, 0, None, :]
    v_im = values[:, 1, None, :]
    w_re = cols_kernel * (v_re * cos_b + v_im * sin_b)
    w_im = cols_kernel * (v_im * cos_b - v_re * sin_b)
    weighted = jnp.stack([w_re, w_im], axis=1)
    patch = jnp.einsum("nak,npbk->napb", rows_kernel, weighted, precision=lax.Precision.HIGHEST)
    return patch.reshape(count, 2 * PATCH * PATCH)


def column_table():
    index = jnp.arange(SG, dtype=jnp.int32)
    phase = index[:, None] * index[None, :] % SG
    angle = phase.astype(jnp.float32) * (2.0 * math.pi / SG)
    scale = 1.0 / math.sqrt(SG)
    cosine = jnp.cos(angle) * scale
    sine = jnp.sin(angle) * scale
    return jnp.concatenate(
        [jnp.concatenate([cosine, -sine], 1), jnp.concatenate([sine, cosine], 1)], 0
    )


def body(
    vis_coords,
    vis_values,
    block_dest,
    block_local,
    block_tile,
    block_counts,
    facet_offsets,
    correction,
):
    n_tm = lax.axis_size("tm")
    n_sub = lax.axis_size("sub")
    devices = n_tm * n_sub
    blocks = vis_coords.shape[0]
    band_rows = SG // n_sub
    band_tiles = band_rows // PATCH
    col_tiles = SG // PATCH
    tiles_all = col_tiles * col_tiles
    chunk = SG // devices
    facet_rows = FS // n_sub

    live = jnp.arange(blocks, dtype=jnp.int32) < block_counts[0]
    patches = make_phased_patches(vis_coords, vis_values, live, block_local)

    target = block_dest[:, 0]
    row_tile = (target % n_sub) * band_tiles + block_tile // col_tiles
    tile_id = row_tile * col_tiles + block_tile % col_tiles
    placer = (
        tile_id[None, :] == jnp.arange(tiles_all, dtype=jnp.int32)[:, None]
    ).astype(jnp.float32)
    tiles = jnp.dot(placer, patches, precision=lax.Precision.HIGHEST)
    per_tile_row = PATCH // chunk
    outgoing = (
        tiles.reshape(col_tiles, col_tiles, per_tile_row, chunk, 2, PATCH)
        .transpose(0, 2, 3, 4, 1, 5)
        .reshape(devices, chunk, 2, SG)
    )
    arrived = lax.all_to_all(
        outgoing, ("tm", "sub"), split_axis=0, concat_axis=0, tiled=True
    )
    grid_rows = jnp.sum(arrived, axis=0).reshape(chunk, 2 * SG)
    spectrum = jnp.dot(grid_rows, column_table(), precision=lax.Precision.HIGHEST).reshape(
        chunk, 2, SG
    )

    offsets = jnp.clip(facet_offsets, 0, SG - FS)
    dest_facet = jnp.arange(devices, dtype=jnp.int32) // n_sub
    columns = offsets[dest_facet, 1][:, None] + jnp.arange(FS, dtype=jnp.int32)[None, :]
    windows = jnp.take(spectrum, columns.reshape(-1), axis=2)
    windows = windows.reshape(chunk, 2, devices, FS).transpose(2, 0, 1, 3)
    gathered = lax.all_to_all(
        windows, ("tm", "sub"), split_axis=0, concat_axis=0, tiled=True
    ).reshape(SG, 2, FS)

    facet = lax.axis_index("tm")
    band = lax.axis_index("sub")
    first_y = offsets[facet, 0] + band * facet_rows
    ys = first_y + jnp.arange(facet_rows, dtype=jnp.int32)
    rs = jnp.arange(SG, dtype=jnp.int32)
    angle = ((ys[:, None] * rs[None, :]) % SG).astype(jnp.float32) * (2.0 * math.pi / SG)
    scale = 1.0 / math.sqrt(SG)
    left = jnp.concatenate([jnp.cos(angle) * scale, jnp.sin(angle) * scale], 1)
    real_part = gathered[:, 0]
    imag_part = gathered[:, 1]
    right = jnp.concatenate(
        [
            jnp.concatenate([real_part, imag_part], 1),
            jnp.concatenate([imag_part, -real_part], 1),
        ],
        0,
    )
    summed = jnp.dot(left, right, precision=lax.Precision.HIGHEST).reshape(
        1, facet_rows, 2, FS
    )
    return summed * correction[:, :, None, :]


def solution(mesh):
    in_specs = (
        P(("tm", "sub"), None, None),
        P(("tm", "sub"), None, None),
        P(("tm", "sub"), None),
        P(("tm", "sub")),
        P(("tm", "sub")),
        P(("tm", "sub")),
        P(),
        P("tm", "sub", None),
    )
    out_specs = P("tm", "sub", None, None)
    return jax.shard_map(body, mesh=mesh, in_specs=in_specs, out_specs=out_specs, check_vma=False)
```

time: 1210 us -> 314 us (0.26); the launches traced: 1190 us -> 313 us
  waiting for transfers between devices: 651 us -> 31.5 us
  loops' own time: 130 us -> 0 us
  matrix products: 189 us -> 91.6 us
  local copies, waits for them, and re-layouts: 162 us -> 147 us
  between operations: 14.7 us -> 1.52 us
    reduce_scatter x1 -> x0, waiting for transfers between devices: 632 us -> none  [body(): lax.psum_scatter(terms.reshape(facet_count * n_sub, facet_rows, 2, FS), (...]
    gather x0 -> x3, local copies, waits for them, and re-layouts: none -> 131 us  [the longest x2 130 us: body(): windows = jnp.take(spectrum, columns.reshape(-1), axis=2)]
    another operation x2 -> x0, loops' own time: 130 us -> none  [the longest x1 129 us: facet_terms(): return lax.map(one_facet, offsets)]
    dot_general x43 -> x4, matrix products: 189 us -> 91.6 us  [the longest x1 79.5 us: make_phased_patches(): jnp.einsum('nak,npbk->napb', rows_kernel, weighted, precision=lax.Precisi...]
    slice x94 -> x1, local copies, waits for them, and re-layouts: 49.7 us -> 2.44 us  [make_phased_patches(): vis_coords[:, 0, None, :] - cells[None, :, None]]
    unnamed x54 -> x8, local copies, waits for them, and re-layouts: 40.6 us -> 0.01 us
    reshape x4 -> x3, local copies, waits for them, and re-layouts: 39.2 us -> 7.91 us  [the longest x1 7.86 us: body(): outgoing = tiles.reshape(col_tiles, col_tiles, per_tile_row, chunk, 2, PA...]
  transfers between devices with their start and end apart: 3 -> 2, of which waited for: 2 -> 2; matrix products, arithmetic and copies ran while one was open for 10% -> 4% of each run, Pallas kernels for 0% -> 0%
where the time goes in v1:
time: 314 us; the launch traced here: 313 us
  local copies, waits for them, and re-layouts  147 us (47%)
  matrix products  91.6 us (29%)
  waiting for transfers between devices  31.5 us (10%)
  other arithmetic  26.7 us (9%)
  starting transfers between devices  15.1 us (5%)
    gather x2, local copies, waits for them, and re-layouts, body(): windows = jnp.take(spectrum, columns.reshape(-1), axis=2)  130 us
    dot_general x1, matrix products, make_phased_patches(): jnp.einsum('nak,npbk->napb', rows_kernel, weighted, precision=lax.Precisi...  79.5 us
    all_to_all x1, waiting for transfers between devices, body(): lax.all_to_all(outgoing, ('tm', 'sub'), split_axis=0, concat_axis=0, tile...  18.8 us
    all_to_all x1, waiting for transfers between devices, body(): lax.all_to_all(windows, ('tm', 'sub'), split_axis=0, concat_axis=0, tiled...  12.7 us
    all_to_all x1, starting transfers between devices, body(): lax.all_to_all(outgoing, ('tm', 'sub'), split_axis=0, concat_axis=0, tile...  11.5 us
    mul x1, other arithmetic, make_phased_patches(): w_re = cols_kernel * (v_re * cos_b + v_im * sin_b)  10.7 us
    reshape x1, local copies, waits for them, and re-layouts, body(): outgoing = tiles.reshape(col_tiles, col_tiles, per_tile_row, chunk, 2, PA...  7.86 us
  transfers between devices with their start and end apart: 2, of which 2 were waited for; matrix products, arithmetic and copies ran while one was open for 4% of the time, Pallas kernels for 0%

profile of v1, /device:TPU:1, one launch (start us, length us, event | category | flops | bytes accessed | tf_op | source)
XLA Modules:
  0.0 313.0 jit_solution(10780069623798630388)
XLA Ops:
  0.0 2.4 fusion.63
  3.1 1.6 copy_select_fusion
  4.7 0.1 slice_bitcast_fusion.1
  4.8 1.0 fusion.49
  5.8 0.2 copy_bitcast_fusion
  6.1 10.7 %add_multiply_fusion = (f32[128,1,32,1024]{3,2,1,0:T(8,128)S(1)}, f32[128,1,32,1024]{3,2,1,0:T(8,128)}) fusion(f32[128,32]{1,0:T(8,128)S(1)} %get-tuple-element.16, f32[128,1024]{1,0:T(8,128)S(1)} %get-tuple-element.10, f32[128,32]{1,0:T(8,128)S(1)} %get-tuple-element.15, f32[128,1024]{1,0:T(8,128)S(1)} %get-tuple-element.9, f32[128,1024]{1,0:T(8,128)S(1)} %get-tuple-element.17), kind=kLoop, calls=%fused_computation.8 | loop fusion | flops 50331648 | bytes 35160064 | tf_op jit(solution)/shard_map/mul | solution.py:34
  16.7 79.5 %fusion = f32[128,32,2,32]{3,1,2,0:T(8,128)} fusion(f32[128,1,32,1024]{3,2,1,0:T(8,128)} %get-tuple-element.6, f32[128,1,32,1024]{3,2,1,0:T(8,128)S(1)} %get-tuple-element.5, f32[128,1024]{1,0:T(8,128)S(1)} %get-tuple-element.18), kind=kOutput, calls=%fused_computation.2 | convolution fusion | flops 3246391296 | bytes 35127296 | tf_op jit(solution)/shard_map/nak,npbk->napb/dot_general | solution.py:37
  96.2 3.8 %copy.19 = f32[128,32,2,32]{0,3,2,1:T(8,128)S(1)} copy(f32[128,32,2,32]{3,1,2,0:T(8,128)} %fusion) | data formatting | bytes 2097152 | tf_op jit(solution)/shard_map/nak,npbk->napb/dot_general | solution.py:37
  100.0 5.6 %convolution_bitcast_fusion = f32[16,8,4,2,16,32]{5,4,3,2,1,0:T(8,128)} fusion(f32[8,4,2,32,128,1]{4,3,2,1,0,5:T(8,128)S(1)} %bitcast.61, s32[16,16]{1,0:T(8,128)S(1)} %multiply_add_fusion, s32[128]{0:T(128)S(1)} %fusion.50), kind=kOutput, calls=%fused_computation.20 | convolution fusion | flops 805339136 | bytes 3147264 | tf_op jit(solution)/shard_map/dot_general | solution.py:83
  105.7 7.9 %reshape.242 = f32[128,4,2,512]{3,2,1,0:T(2,128)} reshape(f32[16,8,4,2,16,32]{5,4,3,2,1,0:T(8,128)} %convolution_bitcast_fusion) | data formatting | bytes 4194304 | tf_op jit(solution)/shard_map/reshape | solution.py:88
  113.5 11.5 %all-to-all-start = ((f32[128,4,2,512]{3,2,1,0:T(2,128)}), f32[128,4,2,512]{3,2,1,0:T(2,128)S(1)}, u32[]{:S(2)}, u32[]{:S(2)}) async-start(f32[128,4,2,512]{3,2,1,0:T(2,128)} %reshape.242), calls=%async_computation | async-start | bytes 4194304 | tf_op jit(solution)/shard_map/all_to_all | solution.py:90
  125.1 1.5 gather_fusion
  126.6 0.1 iota_add_fusion
  126.7 0.1 compare_select_fusion
  126.8 3.9 %fusion.28 = f32[512,512]{0,1:T(8,128)S(1)} fusion(), kind=kLoop, calls=%fused_computation.46 | loop fusion | flops 4194304 | bytes 1048576 | tf_op jit(solution)/shard_map/neg | solution.py:49
  130.6 4.2 %sine_multiply_fusion = (f32[512,512]{0,1:T(8,128)S(1)}, f32[512,512]{0,1:T(8,128)S(1)}) fusion(), kind=kLoop, calls=%fused_computation.36 | loop fusion | flops 4194304 | bytes 2097152 | tf_op jit(solution)/shard_map/mul | solution.py:47
  134.8 2.3 maximum_maximum_fusion
  137.1 0.1 compare_and_fusion
  137.2 18.8 %all-to-all-done = f32[128,4,2,512]{3,2,1,0:T(2,128)S(1)} async-done(((f32[128,4,2,512]{3,2,1,0:T(2,128)}), f32[128,4,2,512]{3,2,1,0:T(2,128)S(1)}, u32[]{:S(2)}, u32[]{:S(2)}) %all-to-all-start) | async-done | bytes 2097184 | tf_op jit(solution)/shard_map/all_to_all | solution.py:90
  156.0 0.8 reduce_sum.9
  156.9 5.9 %fusion.64 = f32[4,2,512]{2,0,1:T(4,128)S(1)} fusion(f32[4,1024,1]{1,0,2:T(4,128)S(1)} %reshape.263, f32[2,512,1024]{2,1,0:T(8,128)} %bitcast.60), kind=kOutput, calls=%fused_computation.116 | convolution fusion | flops 50331648 | bytes 4227072 | tf_op jit(solution)/shard_map/dot_general | solution.py:94
  162.8 0.3 copy.20
  163.1 111.8 %gather_fusion.1 = f32[16384,4,2]{1,2,0:T(2,128)} fusion(f32[4,2,512]{0,1,2:T(2,128)S(1)} %copy.20, s32[16384]{0:T(1024)S(1)} %broadcast_clamp_fusion), kind=kCustom, calls=%fused_computation.1 | custom fusion | bytes 1114112 | tf_op jit(solution)/shard_map/jit(_take)/gather | solution.py:101
  274.8 17.9 %copy.21 = f32[4,2,128,128]{3,0,1,2:T(4,128)S(1)} copy(f32[4,2,128,128]{0,1,3,2:T(2,128)} %bitcast.59) | data formatting | bytes 1048576 | tf_op jit(solution)/shard_map/jit(_take)/gather | solution.py:101
  292.7 1.0 select_bitcast_fusion
  293.7 3.6 %all-to-all-start.1 = ((f32[128,4,2,128]{3,1,2,0:T(4,128)}), f32[128,4,2,128]{3,1,2,0:T(4,128)S(1)}, u32[]{:S(2)}, u32[]{:S(2)}) async-start(f32[128,4,2,128]{3,1,2,0:T(4,128)} %select_bitcast_fusion), calls=%async_computation.1 | async-start | bytes 1048576 | tf_op jit(solution)/shard_map/all_to_all | solution.py:103
  297.3 0.6 constant_dynamic-slice_fusion
  298.6 0.3 cosine_multiply_fusion.1
  298.9 12.7 %all-to-all-done.1 = f32[128,4,2,128]{3,1,2,0:T(4,128)S(1)} async-done(((f32[128,4,2,128]{3,1,2,0:T(4,128)}), f32[128,4,2,128]{3,1,2,0:T(4,128)S(1)}, u32[]{:S(2)}, u32[]{:S(2)}) %all-to-all-start.1) | async-done | bytes 524320 | tf_op jit(solution)/shard_map/all_to_all | solution.py:103
  311.6 0.1 copy.22
  311.8 0.6 fusion.17
  312.4 0.6 broadcast_multiply_fusion
  (19 shorter events, 0.2 us)
Async XLA Ops:
  16.7 83.3 %copy-start.2 = (s32[128,1]{0,1:T(1,128)S(1)}, s32[128,1]{0,1:T(1,128)}, u32[]{:S(2)}) copy-start(s32[128,1]{0,1:T(1,128)} %param.10) | copy-start | bytes 1540
  16.7 83.3 %copy-start.3 = (s32[128]{0:T(128)S(1)}, s32[128]{0:T(128)}, u32[]{:S(2)}) copy-start(s32[128]{0:T(128)} %param.12) | copy-start | bytes 1540
  96.2 28.8 %copy-start.1 = (s32[32,2]{0,1:T(2,128)S(1)}, s32[32,2]{0,1:T(2,128)}, u32[]{:S(2)}) copy-start(s32[32,2]{0,1:T(2,128)} %param.14) | copy-start | bytes 772
  113.5 42.5 %all-to-all-start = ((f32[128,4,2,512]{3,2,1,0:T(2,128)}), f32[128,4,2,512]{3,2,1,0:T(2,128)S(1)}, u32[]{:S(2)}, u32[]{:S(2)}) async-start(f32[128,4,2,512]{3,2,1,0:T(2,128)} %reshape.242), calls=%async_computation | async-start | bytes 4194304 | tf_op jit(solution)/shard_map/all_to_all | solution.py:90
  137.1 175.3 %copy-start = (f32[1,32,128]{2,1,0:T(8,128)S(1)}, f32[1,32,128]{2,1,0:T(8,128)}, u32[]{:S(2)}) copy-start(f32[1,32,128]{2,1,0:T(8,128)} %param.15) | copy-start | bytes 49156
  293.7 17.9 %all-to-all-start.1 = ((f32[128,4,2,128]{3,1,2,0:T(4,128)}), f32[128,4,2,128]{3,1,2,0:T(4,128)S(1)}, u32[]{:S(2)}, u32[]{:S(2)}) async-start(f32[128,4,2,128]{3,1,2,0:T(4,128)} %select_bitcast_fusion), calls=%async_computation.1 | async-start | bytes 1048576 | tf_op jit(solution)/shard_map/all_to_all | solution.py:103
